TPU v7x, 128 devices: a whole 4x4x4 slice. The times are simulated.
128 devices in a mesh: segment: 8 (over x, core), blk: 16 (over y, z).
Axes of the slice: x: 4, y: 4, z: 4, core: 2. Of those that a mesh axis runs over, the one named last changes fastest.
Arguments:
- fresh: bfloat16 [256, 4096], replicated, may hold values from -6 to 6
- previous: bfloat16 [8, 256, 4096], P('segment'), may hold values from -6 to 6
- span_index: int32 [8], P('segment'), may hold values from 0 to 7
- cache_counts: int32 [8, 16], P('segment'), may hold values from 1 to 2048, 16384 in all within a row
- norm_gain: float32 [8, 4096], P('segment'), may hold values from 0.1 to 1.9
- w_query: bfloat16 [8, 4096, 4096], P('segment', None, 'blk'), may hold values from -0.375 to 0.375
- w_keyval: bfloat16 [8, 4096, 2048], P('segment', None, 'blk'), may hold values from -0.09375 to 0.09375
- w_out: bfloat16 [8, 4096, 4096], P('segment', 'blk'), may hold values from -0.09375 to 0.09375
- cache_keys: bfloat16 [8, 32768, 1024], P('segment', 'blk'), may hold values from -220 to 220
- cache_values: bfloat16 [8, 32768, 1024], P('segment', 'blk'), may hold values from -6 to 6
Outputs:
- mixed: bfloat16 [8, 256, 4096], P('segment')
Inputs may be any that keep to these rules, and one draw needn't show every extreme that they name: Each row of cache_counts sums to 16384 and its largest entry is 2048.
All inputs are finite; a program needn't handle non-finite values.
Results may differ from a plain program's by a relative error of at most 0.012.
Values may be sent and summed in bfloat16 or wider, within the bound.
No kernel may reach another device: no remote copies, remote signals or barrier semaphores. Data moves between devices by JAX's collectives and lax.ppermute only.
A program may use at most 128 MiB of HBM per device.

v0:
```python
import jax
import jax.numpy as jnp
from jax import lax
from jax.sharding import PartitionSpec as P

KVH = 8
HD = 128
ROPE_BASE = 500000.0
EPSILON = 1e-05


def passed_along(block, axis, distance):
    devices = range(lax.axis_size(axis))
    route = [(i - distance, i) for i in devices if i - distance in devices]
    return lax.ppermute(block, axis, route)


def swapped(block, axis, distance):
    count = lax.axis_size(axis)
    route = []
    for low in range(count):
        high = low | 1 << distance
        if high != low and high < count:
            route += [(low, high), (high, low)]
    return lax.ppermute(block, axis, route)


def rotate(projected, first_span):
    length = projected.shape[0]
    half_width = projected.shape[-1] // 2
    positions = (first_span * length + jnp.arange(length, dtype=jnp.int32)).astype(jnp.float32)
    inverse = ROPE_BASE ** (
        -(jnp.arange(half_width, dtype=jnp.float32) * 2.0) / projected.shape[-1]
    )
    angles = positions[:, None] * inverse[None, :]
    cosine = jnp.cos(angles)[:, None, :]
    sine_table = jnp.sin(angles)[:, None, :]
    left_part = projected[..., :half_width]
    right_part = projected[..., half_width:]
    return jnp.concatenate(
        [
            left_part * cosine - right_part * sine_table,
            right_part * cosine + left_part * sine_table,
        ],
        axis=-1,
    )


def attend_rows(query_rows, key_rows, value_rows, allowed):
    scores = lax.dot_general(
        query_rows, key_rows, (((1,), (1,)), ((), ())), preferred_element_type=jnp.float32
    ) * query_rows.shape[-1] ** (-0.5)
    scores = jnp.where(allowed, scores, -jnp.inf)
    highest = jnp.max(scores, axis=-1, keepdims=True)
    weights = jnp.exp(scores - highest)
    totals = jnp.sum(weights, axis=-1, keepdims=True)
    partial_out = (
        jnp.dot(weights.astype(jnp.bfloat16), value_rows, preferred_element_type=jnp.float32)
        / totals
    ).astype(jnp.bfloat16)
    return (partial_out, (highest + jnp.log(totals))[:, 0])


def shards(
    fresh,
    previous,
    span_index,
    cache_counts,
    norm_gain,
    w_query,
    w_keyval,
    w_out,
    cache_keys,
    cache_values,
):
    blocks = lax.axis_size("blk")
    position = lax.axis_index("blk")
    span_rows = fresh.shape[0]
    arrived = passed_along(previous[0], "segment", 1)
    current = jnp.where(lax.axis_index("segment") == 0, fresh, arrived)
    widened = current.astype(jnp.float32)
    normed = (
        widened
        * lax.rsqrt(jnp.mean(widened * widened, axis=-1, keepdims=True) + EPSILON)
        * norm_gain[0]
    ).astype(jnp.bfloat16)
    first_span = span_index[0]
    heads_here = w_query.shape[2] // HD
    ratio = blocks // KVH
    queries = jnp.dot(normed, w_query[0], preferred_element_type=jnp.float32).reshape(
        span_rows, heads_here, HD
    )
    queries = rotate(queries, first_span).astype(jnp.bfloat16).reshape(span_rows, heads_here * HD)
    projected = jnp.dot(normed, w_keyval[0], preferred_element_type=jnp.float32)
    odd_member = position % 2 == 1
    as_key = rotate(projected[:, None, :], first_span)[:, 0, :].astype(jnp.bfloat16)
    mine = jnp.where(odd_member, projected.astype(jnp.bfloat16), as_key)
    partner = swapped(mine, "blk", 0)
    own_keys = jnp.where(odd_member, partner, mine)
    own_values = jnp.where(odd_member, mine, partner)
    query_rows = queries.reshape(span_rows * heads_here, HD)
    row_tokens = jnp.arange(span_rows * heads_here, dtype=jnp.int32) // heads_here
    causal = row_tokens[:, None] >= jnp.arange(span_rows, dtype=jnp.int32)[None, :]
    own_out, own_log = attend_rows(query_rows, own_keys, own_values, causal)
    own_out = own_out.reshape(span_rows, heads_here * HD)
    own_log = own_log.reshape(span_rows, heads_here).T
    cache_rows = cache_keys.shape[1]
    offsets = jnp.arange(cache_rows, dtype=jnp.int32)
    every_query = lax.all_gather(queries, "blk", axis=0, tiled=True)
    live = cache_counts[0, position]

    def holder(source):
        query_block = lax.dynamic_slice_in_dim(
            every_query, source * span_rows, span_rows, 0
        ).reshape(span_rows * heads_here, HD)
        head_start = source // ratio * HD
        key_rows = lax.dynamic_slice_in_dim(cache_keys[0], head_start, HD, 1)
        value_rows = lax.dynamic_slice_in_dim(cache_values[0], head_start, HD, 1)
        partial_out, log_totals = attend_rows(
            query_block, key_rows, value_rows, (offsets < live)[None, :]
        )
        return (
            partial_out.reshape(span_rows, heads_here * HD),
            log_totals.reshape(span_rows, heads_here).T,
        )

    held_outs, held_logs = lax.map(holder, jnp.arange(blocks, dtype=jnp.int32))
    shard_outs = lax.all_to_all(held_outs, "blk", split_axis=0, concat_axis=0, tiled=True)
    shard_logs = lax.all_to_all(held_logs, "blk", split_axis=0, concat_axis=0, tiled=True)
    all_outs = (
        jnp.concatenate([own_out[None], shard_outs], axis=0)
        .astype(jnp.float32)
        .reshape(blocks + 1, span_rows, heads_here, HD)
    )
    all_logs = jnp.concatenate([own_log[None], shard_logs], axis=0).transpose(0, 2, 1)
    ceiling = jnp.max(all_logs, axis=0)
    factors = jnp.exp(all_logs - ceiling)
    attended = (
        jnp.sum(factors[..., None] * all_outs, axis=0) / jnp.sum(factors, axis=0)[..., None]
    ).astype(jnp.bfloat16)
    attended = attended.reshape(span_rows, heads_here * HD)
    head_terms = lax.optimization_barrier(
        jnp.dot(attended, w_out[0], preferred_element_type=jnp.float32).astype(jnp.bfloat16)
    ).astype(jnp.float32)
    summed = lax.psum(head_terms.astype(jnp.bfloat16), "blk").astype(jnp.float32)
    mixed = (widened + summed).astype(jnp.bfloat16)
    return mixed[None]


def solution(mesh):
    placed = (
        P(),
        P("segment", None, None),
        P("segment"),
        P("segment", None),
        P("segment", None),
        P("segment", None, "blk"),
        P("segment", None, "blk"),
        P("segment", "blk", None),
        P("segment", "blk", None),
        P("segment", "blk", None),
    )
    return jax.shard_map(
        shards, mesh=mesh, in_specs=placed, out_specs=P("segment", None, None), check_vma=False
    )
```

profile of v0, /device:TPU:0, one launch (start us, length us, event | category | flops | bytes accessed | tf_op | source)
XLA Modules:
  0.0 425.8 jit_solution(5192613194957220926)
XLA Ops:
  6.5 2.8 collective-permute-start
  9.3 4.1 copy.33
  14.4 2.7 fusion.23
  19.9 67.0 %all-gather.2.cloned.1.call-done = bf16[4096,256]{1,0:T(8,128)(2,1)} async-done(((bf16[256,256]{1,0:T(8,128)(2,1)}), bf16[4096,256]{1,0:T(8,128)(2,1)}) %all-gather.2.cloned.1.call-update) | async-done | bytes 2097168 | tf_op jit(solution)/shard_map/all_gather | solution.py:109
  87.0 177.8 %while.15 = (s32[]{:T(128)}, bf16[16,256,256]{2,1,0:T(8,128)(2,1)}, f32[16,2,256]{2,1,0:T(2,128)S(1)}, s32[]{:T(128)}, s32[16]{0:T(128)S(1)}, /*index=5*/bf16[40...) while((s32[]{:T(128)}, bf16[16,256,256]{2,1,0:T(8,128)(2,1)}, ...), condition=%wide.region_6.7_spmd.clone, body=%wide.region_3.6_spmd.clone.sunk | while | flops 548537856 | bytes 14979499 | solution.py:127
  106.2 2.0 fusion.79
  117.3 2.0 fusion.79
  139.5 2.0 fusion.79
  150.6 2.0 fusion.79
  172.9 2.0 fusion.79
  206.2 2.0 fusion.79
  217.3 2.0 fusion.79
  239.6 2.0 fusion.79
  250.7 2.0 fusion.79
  264.8 12.4 %all_to_all.10 = f32[16,2,256]{2,1,0:T(2,128)S(1)} all-to-all(f32[16,2,256]{2,1,0:T(2,128)S(1)} %get-tuple-element.120), channel_id=1, replica_groups=mesh['segment'=8,'blk'=16] {'blk'}, dimensions={0} | all-to-all | bytes 65536 | tf_op jit(solution)/shard_map/all_to_all | solution.py:129
  277.2 4.4 %all-to-all-start.1 = ((bf16[16,256,256]{2,1,0:T(8,128)(2,1)}), bf16[16,256,256]{2,1,0:T(8,128)(2,1)}, u32[]{:S(2)}, u32[]{:S(2)}) async-start(bf16[16,256,256]{2,1,0:T(8,128)(2,1)} %get-tuple-element.121), calls=%async_computation.1 | async-start | bytes 4194304 | tf_op jit(solution)/shard_map/all_to_all | solution.py:128
  281.6 2.8 fusion.33
  286.9 18.0 %collective-permute-done.1 = bf16[256,128]{0,1:T(8,128)(2,1)S(1)} collective-permute-done((bf16[256,128]{0,1:T(8,128)(2,1)S(1)}, bf16[256,128]{0,1:T(8,128)(2,1)S(1)}, u32[]{:S(2)}, u32[]{:S(2)}) %collective-permute-start.1) | collective-permute-done | bytes 65568 | tf_op jit(solution)/shard_map/ppermute | solution.py:25
  306.0 2.1 copy.31
  309.4 4.0 concatenate.34
  313.4 7.7 %multiply_reduce_fusion = f32[256,2,128]{2,1,0:T(2,128)S(1)} fusion(bf16[16,256,2,128]{3,2,1,0:T(2,128)(2,1)} %concatenate.34, bf16[1,256,2,128]{3,2,1,0:T(2,128)(2,1)S(1)} %bitcast.73, f32[17,256,2]{2,1,0:T(8,128)} %copy.31), kind=kLoop, calls=%fused_computation.28 | loop fusion | flops 4390912 | bytes 2525184 | tf_op jit(solution)/shard_map/reduce_sum | solution.py:139
  321.5 2.0 convolution_convert_fusion
  323.5 91.1 %all-reduce.2.cloned.1.call-done = bf16[256,4096]{1,0:T(8,128)(2,1)} async-done(((bf16[256,4096]{1,0:T(8,128)(2,1)}), bf16[256,4096]{1,0:T(8,128)(2,1)}) %all-reduce.2.cloned.1.call-update) | async-done | bytes 2097168 | tf_op jit(solution)/shard_map/psum | solution.py:145
  414.6 4.3 %fusion.27 = bf16[1,256,4096]{2,1,0:T(8,128)(2,1)} fusion(bf16[256,4096]{1,0:T(8,128)(2,1)} %all-reduce.2.cloned.1.call-done, bf16[256,4096]{1,0:T(8,128)(2,1)} %copy-done.1), kind=kLoop, calls=%fused_computation.33 | loop fusion | flops 4194304 | bytes 6291456 | tf_op jit(solution)/shard_map/broadcast_in_dim | solution.py:147
  (243 shorter events, 117.4 us)
Async XLA Ops:
  6.5 314.9 %copy-start = (bf16[1,256,4096]{2,1,0:T(8,128)(2,1)S(1)}, bf16[1,256,4096]{2,1,0:T(8,128)(2,1)}, u32[]{:S(2)}) copy-start(bf16[1,256,4096]{2,1,0:T(8,128)(2,1)} %param.19) | copy-start | bytes 6291460
  6.5 80.4 %all-gather.2.cloned.1.call-start = ((), (), s32[]{:S(2)}) async-start(), calls=%async_computation.2 | async-start | bytes 2228224 | tf_op jit(solution)/shard_map/all_gather | solution.py:109
  6.5 7.9 %collective-permute-start = (bf16[256,4096]{1,0:T(8,128)(2,1)}, bf16[256,4096]{1,0:T(8,128)(2,1)}, u32[]{:S(2)}, u32[]{:S(2)}) collective-permute-start(bf16[256,4096]{1,0:T(8,128)(2,1)} %bitcast.76), channel_id=1, source_target_pairs={{0,16},{16,32},{32,48},{48,64},{64,80},{80,96},{96,112},{1,17},{17... | collective-permute-start | bytes 6291464 | tf_op jit(solution)/shard_map/ppermute | solution.py:15
  14.4 2.8 copy-start.2
  14.4 2.8 copy-start.3
  17.1 1.3 copy-start.1
  17.2 2.1 copy-start.4
  277.2 32.3 %all-to-all-start.1 = ((bf16[16,256,256]{2,1,0:T(8,128)(2,1)}), bf16[16,256,256]{2,1,0:T(8,128)(2,1)}, u32[]{:S(2)}, u32[]{:S(2)}) async-start(bf16[16,256,256]{2,1,0:T(8,128)(2,1)} %get-tuple-element.121), calls=%async_computation.1 | async-start | bytes 4194304 | tf_op jit(solution)/shard_map/all_to_all | solution.py:128
  281.6 133.0 %all-reduce.2.cloned.1.call-start = ((), (), s32[]{:S(2)}) async-start(), calls=%async_computation.3 | async-start | bytes 4194304 | tf_op jit(solution)/shard_map/psum | solution.py:145
  284.8 20.1 %collective-permute-start.1 = (bf16[256,128]{0,1:T(8,128)(2,1)S(1)}, bf16[256,128]{0,1:T(8,128)(2,1)S(1)}, u32[]{:S(2)}, u32[]{:S(2)}) collective-permute-start(bf16[256,128]{0,1:T(8,128)(2,1)S(1)} %fusion.54), channel_id=1, source_target_pairs={{0,1},{1,0},{2,3},{3,2},{4,5},{5,4},{6,7},{7,6},{8,9},{9,8},{10,11... | collective-permute-start | bytes 196616 | tf_op jit(solution)/shard_map/ppermute | solution.py:25
Sparse Core Ops, SparseCore 0:
  19.4 67.5 all-gather.1
  323.6 90.9 all-reduce.1
where the time goes:
time: 429 us; the launch traced here: 426 us
  waiting for transfers between devices  177 us (41%)
  matrix products  68.5 us (16%)
  local copies, waits for them, and re-layouts  52.7 us (12%)
  loops' own time  50.4 us (12%)
  other arithmetic  41.1 us (10%)
  between operations  14.3 us (3%)
  blocking collectives  12.4 us (3%)
  starting transfers between devices  9.06 us (2%)
    psum x1, waiting for transfers between devices, shards(): lax.psum(head_terms.astype(jnp.bfloat16), 'blk').astype(jnp.float32)  91.1 us
    all_gather x1, waiting for transfers between devices, shards(): every_query = lax.all_gather(queries, 'blk', axis=0, tiled=True)  67 us
    another operation x1, loops' own time, shards(): held_outs, held_logs = lax.map(holder, jnp.arange(blocks, dtype=jnp.int32))  50.4 us
    dot_general x17, matrix products, attend_rows(): jnp.dot(weights.astype(jnp.bfloat16), value_rows, preferred_element_type=...  32.6 us
    dot_general x17, matrix products, attend_rows(): lax.dot_general(query_rows, key_rows, (((1,), (1,)), ((), ())), preferred...  30.1 us
    ppermute x1, waiting for transfers between devices, swapped(): return lax.ppermute(block, axis, route)  18 us
    reduce_sum x17, other arithmetic, attend_rows(): totals = jnp.sum(weights, axis=-1, keepdims=True)  15.2 us
    dynamic_slice x16, local copies, waits for them, and re-layouts, holder(): lax.dynamic_slice_in_dim(every_query, source * span_rows, span_rows, 0)  14.7 us
  transfers between devices with their start and end apart: 5, of which 4 were waited for; matrix products, arithmetic and copies ran while one was open for 3% of the time, Pallas kernels for 0%

commit v1 on v0

--- a/solution.py
+++ b/solution.py
@@ -106,7 +106,16 @@
     own_log = own_log.reshape(span_rows, heads_here).T
     cache_rows = cache_keys.shape[1]
     offsets = jnp.arange(cache_rows, dtype=jnp.int32)
-    every_query = lax.all_gather(queries, "blk", axis=0, tiled=True)
+    convert_rings = lambda inner_x: jnp.concatenate(
+        lax.all_to_all(
+            jnp.stack([inner_x] * lax.axis_size("blk")),
+            axis_name="blk",
+            split_axis=0,
+            concat_axis=0,
+        ),
+        axis=0,
+    )
+    every_query = convert_rings(queries)
     live = cache_counts[0, position]
 
     def holder(source):

time: 429 us -> 415 us (0.967)
  waiting for transfers between devices: 177 us -> 155 us
  starting transfers between devices: 9.06 us -> 18 us
    all_gather x1 -> x0, waiting for transfers between devices: 67 us -> none  [shards(): every_query = lax.all_gather(queries, 'blk', axis=0, tiled=True)]
    psum x1, waiting for transfers between devices: 91.1 us -> 125 us  [shards(): lax.psum(head_terms.astype(jnp.bfloat16), 'blk').astype(jnp.float32)]
    all_to_all x0 -> x1, waiting for transfers between devices: none -> 18.9 us  [shards(): lax.all_to_all(jnp.stack([inner_x] * lax.axis_size('blk')), axis_name='bl...]
    all_to_all x0 -> x1, starting transfers between devices: none -> 8.76 us  [shards(): lax.all_to_all(jnp.stack([inner_x] * lax.axis_size('blk')), axis_name='bl...]
    ppermute x1, waiting for transfers between devices: 18 us -> 9.47 us  [swapped(): return lax.ppermute(block, axis, route)]
where the time goes in v1:
time: 415 us; the launch traced here: 412 us
  waiting for transfers between devices  155 us (37%)
  matrix products  68.5 us (17%)
  local copies, waits for them, and re-layouts  53.5 us (13%)
  loops' own time  50.5 us (12%)
  other arithmetic  41.1 us (10%)
  starting transfers between devices  18 us (4%)
  between operations  14.3 us (3%)
  blocking collectives  11.3 us (3%)
    psum x1, waiting for transfers between devices, shards(): lax.psum(head_terms.astype(jnp.bfloat16), 'blk').astype(jnp.float32)  125 us
    another operation x1, loops' own time, shards(): held_outs, held_logs = lax.map(holder, jnp.arange(blocks, dtype=jnp.int32))  50.5 us
    dot_general x17, matrix products, attend_rows(): jnp.dot(weights.astype(jnp.bfloat16), value_rows, preferred_element_type=...  32.6 us
    dot_general x17, matrix products, attend_rows(): lax.dot_general(query_rows, key_rows, (((1,), (1,)), ((), ())), preferred...  30.2 us
    all_to_all x1, waiting for transfers between devices, shards(): lax.all_to_all(jnp.stack([inner_x] * lax.axis_size('blk')), axis_name='bl...  18.9 us
    reduce_sum x17, other arithmetic, attend_rows(): totals = jnp.sum(weights, axis=-1, keepdims=True)  15.2 us
    dynamic_slice x16, local copies, waits for them, and re-layouts, holder(): lax.dynamic_slice_in_dim(every_query, source * span_rows, span_rows, 0)  14.7 us
    dynamic_update_slice x48, local copies, waits for them, and re-layouts, shards(): held_outs, held_logs = lax.map(holder, jnp.arange(blocks, dtype=jnp.int32))  12.2 us
  transfers between devices with their start and end apart: 5, of which 4 were waited for; matrix products, arithmetic and copies ran while one was open for 3% of the time, Pallas kernels for 0%

profile of v1, /device:TPU:0, one launch (start us, length us, event | category | flops | bytes accessed | tf_op | source)
XLA Modules:
  0.0 412.0 jit_solution(13070000664983280524)
XLA Ops:
  6.5 2.8 collective-permute-start
  10.0 4.1 copy.33
  14.4 2.7 fusion.23
  20.1 8.8 %all-to-all-start = ((bf16[16,256,256]{2,1,0:T(8,128)(2,1)}), bf16[16,256,256]{2,1,0:T(8,128)(2,1)}, u32[]{:S(2)}, u32[]{:S(2)}) async-start(bf16[16,256,256]{2,1,0:T(8,128)(2,1)} %stack.3), calls=%async_computation | async-start | bytes 4194304 | tf_op jit(solution)/shard_map/all_to_all | solution.py:110
  29.5 18.9 %all-to-all-done = bf16[16,256,256]{2,1,0:T(8,128)(2,1)} async-done(((bf16[16,256,256]{2,1,0:T(8,128)(2,1)}), bf16[16,256,256]{2,1,0:T(8,128)(2,1)}, u32[]{:S(2)}, u32[]{:S(2)}) %all-to-all-start) | async-done | bytes 2097184 | tf_op jit(solution)/shard_map/all_to_all | solution.py:110
  48.4 177.9 %while.15 = (s32[]{:T(128)}, bf16[16,256,256]{2,1,0:T(8,128)(2,1)}, f32[16,2,256]{2,1,0:T(2,128)S(1)}, s32[]{:T(128)}, s32[16]{0:T(128)S(1)}, /*index=5*/bf16[40...) while((s32[]{:T(128)}, bf16[16,256,256]{2,1,0:T(8,128)(2,1)}, ...), condition=%wide.region_6.7_spmd.clone, body=%wide.region_3.6_spmd.clone.sunk | while | flops 548537856 | bytes 14979499 | solution.py:136
  67.6 2.0 fusion.79
  78.7 2.0 fusion.79
  101.0 2.0 fusion.79
  123.2 2.0 fusion.79
  145.4 2.0 fusion.79
  178.8 2.0 fusion.79
  189.9 2.0 fusion.79
  223.2 2.0 fusion.79
  226.2 11.3 %all_to_all.15 = f32[16,2,256]{2,1,0:T(2,128)S(1)} all-to-all(f32[16,2,256]{2,1,0:T(2,128)S(1)} %get-tuple-element.120), channel_id=1, replica_groups=mesh['segment'=8,'blk'=16] {'blk'}, dimensions={0} | all-to-all | bytes 65536 | tf_op jit(solution)/shard_map/all_to_all | solution.py:138
  237.5 4.4 %all-to-all-start.2 = ((bf16[16,256,256]{2,1,0:T(8,128)(2,1)}), bf16[16,256,256]{2,1,0:T(8,128)(2,1)}, u32[]{:S(2)}, u32[]{:S(2)}) async-start(bf16[16,256,256]{2,1,0:T(8,128)(2,1)} %get-tuple-element.121), calls=%async_computation.2 | async-start | bytes 4194304 | tf_op jit(solution)/shard_map/all_to_all | solution.py:137
  242.0 2.8 fusion.33
  247.4 9.5 %collective-permute-done.1 = bf16[256,128]{0,1:T(8,128)(2,1)S(1)} collective-permute-done((bf16[256,128]{0,1:T(8,128)(2,1)S(1)}, bf16[256,128]{0,1:T(8,128)(2,1)S(1)}, u32[]{:S(2)}, u32[]{:S(2)}) %collective-permute-start.1) | collective-permute-done | bytes 65568 | tf_op jit(solution)/shard_map/ppermute | solution.py:25
  258.1 2.1 copy.31
  261.5 4.0 concatenate.34
  265.5 7.7 %multiply_reduce_fusion = f32[256,2,128]{2,1,0:T(2,128)S(1)} fusion(bf16[16,256,2,128]{3,2,1,0:T(2,128)(2,1)} %concatenate.34, bf16[1,256,2,128]{3,2,1,0:T(2,128)(2,1)S(1)} %bitcast.74, f32[17,256,2]{2,1,0:T(8,128)} %copy.31), kind=kLoop, calls=%fused_computation.28 | loop fusion | flops 4390912 | bytes 2525184 | tf_op jit(solution)/shard_map/reduce_sum | solution.py:148
  273.6 2.0 convolution_convert_fusion
  275.6 125.2 %all-reduce.2.cloned.1.call-done = bf16[256,4096]{1,0:T(8,128)(2,1)} async-done(((bf16[256,4096]{1,0:T(8,128)(2,1)}), bf16[256,4096]{1,0:T(8,128)(2,1)}) %all-reduce.2.cloned.1.call-update) | async-done | bytes 2097168 | tf_op jit(solution)/shard_map/psum | solution.py:154
  400.8 4.3 %fusion.27 = bf16[1,256,4096]{2,1,0:T(8,128)(2,1)} fusion(bf16[256,4096]{1,0:T(8,128)(2,1)} %all-reduce.2.cloned.1.call-done, bf16[256,4096]{1,0:T(8,128)(2,1)} %copy-done.1), kind=kLoop, calls=%fused_computation.33 | loop fusion | flops 4194304 | bytes 6291456 | tf_op jit(solution)/shard_map/broadcast_in_dim | solution.py:156
  (243 shorter events, 120.6 us)
Async XLA Ops:
  6.5 267.0 %copy-start = (bf16[1,256,4096]{2,1,0:T(8,128)(2,1)S(1)}, bf16[1,256,4096]{2,1,0:T(8,128)(2,1)}, u32[]{:S(2)}) copy-start(bf16[1,256,4096]{2,1,0:T(8,128)(2,1)} %param.19) | copy-start | bytes 6291460
  6.5 7.9 %collective-permute-start = (bf16[256,4096]{1,0:T(8,128)(2,1)}, bf16[256,4096]{1,0:T(8,128)(2,1)}, u32[]{:S(2)}, u32[]{:S(2)}) collective-permute-start(bf16[256,4096]{1,0:T(8,128)(2,1)} %bitcast.77), channel_id=1, source_target_pairs={{0,16},{16,32},{32,48},{48,64},{64,80},{80,96},{96,112},{1,17},{17... | collective-permute-start | bytes 6291464 | tf_op jit(solution)/shard_map/ppermute | solution.py:15
  14.4 2.8 copy-start.2
  14.4 2.8 copy-start.3
  17.1 1.3 copy-start.1
  20.1 8.8 %copy-start.4 = (s32[1,16]{1,0:T(1,128)S(1)}, s32[1,16]{1,0:T(1,128)}, u32[]{:S(2)}) copy-start(s32[1,16]{1,0:T(1,128)} %param.15) | copy-start | bytes 196
  20.1 28.3 %all-to-all-start = ((bf16[16,256,256]{2,1,0:T(8,128)(2,1)}), bf16[16,256,256]{2,1,0:T(8,128)(2,1)}, u32[]{:S(2)}, u32[]{:S(2)}) async-start(bf16[16,256,256]{2,1,0:T(8,128)(2,1)} %stack.3), calls=%async_computation | async-start | bytes 4194304 | tf_op jit(solution)/shard_map/all_to_all | solution.py:110
  237.5 24.0 %all-to-all-start.2 = ((bf16[16,256,256]{2,1,0:T(8,128)(2,1)}), bf16[16,256,256]{2,1,0:T(8,128)(2,1)}, u32[]{:S(2)}, u32[]{:S(2)}) async-start(bf16[16,256,256]{2,1,0:T(8,128)(2,1)} %get-tuple-element.121), calls=%async_computation.2 | async-start | bytes 4194304 | tf_op jit(solution)/shard_map/all_to_all | solution.py:137
  241.9 158.9 %all-reduce.2.cloned.1.call-start = ((), (), s32[]{:S(2)}) async-start(), calls=%async_computation.3 | async-start | bytes 4194304 | tf_op jit(solution)/shard_map/psum | solution.py:154
  245.2 11.7 %collective-permute-start.1 = (bf16[256,128]{0,1:T(8,128)(2,1)S(1)}, bf16[256,128]{0,1:T(8,128)(2,1)S(1)}, u32[]{:S(2)}, u32[]{:S(2)}) collective-permute-start(bf16[256,128]{0,1:T(8,128)(2,1)S(1)} %fusion.54), channel_id=1, source_target_pairs={{0,1},{1,0},{2,3},{3,2},{4,5},{5,4},{6,7},{7,6},{8,9},{9,8},{10,11... | collective-permute-start | bytes 196616 | tf_op jit(solution)/shard_map/ppermute | solution.py:25
Sparse Core Ops, SparseCore 0:
  275.8 124.9 all-reduce.1
